TPU v7x, 256 devices: a whole 4x4x8 slice. The times are simulated.
256 devices in a mesh: fsdp: 32 (over y, x, z_hi), tp: 8 (over z_lo, core).
Axes of the slice: x: 4, y: 4, z: 8 (z_hi: 2, z_lo: 4; z = z_hi * 4 + z_lo), core: 2. Of those that a mesh axis runs over, the one named last changes fastest.
Arguments:
- tokens: bfloat16 [16384, 4096], P(('fsdp', 'tp')), may hold values from -6 to 6
- in_weight: bfloat16 [4096, 3, 4096], P('fsdp', None, 'tp'), may hold values from -0.09375 to 0.09375
- out_weight: bfloat16 [4096, 4096], P('fsdp', 'tp'), may hold values from -0.09375 to 0.09375
- short_taps: float32 [3, 3, 4096], P(None, None, 'tp'), may hold values from -3 to 3
- filter_taps: float32 [128, 4096], P(None, 'tp'), may hold values from -1.2 to 1.2
- decay_rate: float32 [4096], P('tp'), may hold values from 0.00390625 to 0.09375
- doc_lengths: int32 [64], replicated, may hold values from 1 to 2048, 16384 in all
Outputs:
- mixed_out: bfloat16 [16384, 4096], P(('fsdp', 'tp'))
Inputs may be any that keep to these rules, and one draw needn't show every extreme that they name: `doc_lengths`: the documents of the window in order; they sum to 16384.
All inputs are finite; a program needn't handle non-finite values.
Results may differ from a plain program's by a relative error of at most 0.014.
Values may be sent and summed in bfloat16 or wider, within the bound.
No kernel may reach another device: no remote copies, remote signals or barrier semaphores. Data moves between devices by JAX's collectives and lax.ppermute only.
A program may use at most 64 MiB of HBM per device.

v0:
```python
import jax
import jax.numpy as jnp
from jax import lax
from jax.sharding import Mesh
from jax.sharding import PartitionSpec as P

COL = ("zh", "zl", "c")


def doc_position(points, lengths):
    starts = jnp.cumsum(lengths) - lengths
    begins = jnp.max(jnp.where(starts[None, :] <= points[:, None], starts[None, :], 0), axis=1)
    return points - begins


def short_filter(extended, short_taps, positions, out_count):
    running = jnp.zeros((out_count,) + extended.shape[1:], jnp.float32)
    for tap_index in range(3):
        window = extended[2 - tap_index : 2 - tap_index + out_count].astype(jnp.float32)
        inside = (positions >= tap_index)[:, None, None]
        running = running + jnp.where(
            inside, short_taps[tap_index][None] * window, jnp.float32(0.0)
        )
    return running


def long_filter(extended, shaped, positions, out_count, tap_count):

    def tap_group(group_index, running):
        for inner in range(16):
            tap_index = group_index * 16 + inner
            window = lax.dynamic_slice_in_dim(extended, tap_count - tap_index, out_count, 0)
            weight_row = lax.dynamic_slice_in_dim(shaped, tap_index, 1, 0)
            inside = (positions >= tap_index)[:, None]
            running = running + jnp.where(
                inside, weight_row * window.astype(jnp.float32), jnp.float32(0.0)
            )
        return running

    zero_sum = jnp.zeros((out_count, shaped.shape[1]), jnp.float32)
    return lax.fori_loop(0, tap_count // 16, tap_group, zero_sum)


def swap_half(piece, zh, axis):
    width = piece.shape[axis] // 2
    lo = lax.slice_in_dim(piece, 0, width, axis=axis)
    hi = lax.slice_in_dim(piece, width, 2 * width, axis=axis)
    keep = jnp.where(zh == 0, lo, hi)
    give = jnp.where(zh == 0, hi, lo)
    got = lax.ppermute(give, "zh", [(0, 1), (1, 0)])
    first = jnp.where(zh == 0, keep, got)
    second = jnp.where(zh == 0, got, keep)
    return jnp.concatenate([first, second], 0)


def body(tokens, in_weight, out_weight, short_taps, filter_taps, decay_rate, doc_lengths):
    zh = lax.axis_index("zh")
    col_size = lax.axis_size("zh") * lax.axis_size("zl") * lax.axis_size("c")
    own_rows = tokens.shape[0]
    col_rows = own_rows * col_size
    half = in_weight.shape[2] // 2
    tap_count = filter_taps.shape[0]
    widened = tokens.astype(jnp.float32)
    normed = (
        widened * lax.rsqrt(jnp.mean(widened * widened, axis=1, keepdims=True) + 1e-06)
    ).astype(jnp.bfloat16)
    gathered = lax.all_gather(normed, COL, axis=0, tiled=True)
    in_piece = swap_half(in_weight, zh, 2)
    in_full = lax.all_gather(in_piece, "p", axis=0, tiled=True)
    out_piece = swap_half(out_weight, zh, 1)
    out_full = lax.all_gather(out_piece, "p", axis=0, tiled=True)
    flat_in = in_full.reshape(in_full.shape[0], 3 * half)
    projected = jnp.dot(gathered, flat_in, preferred_element_type=jnp.float32)
    projected = projected.astype(jnp.bfloat16).reshape(col_rows, 3, half)
    first_row = lax.axis_index("p") * col_rows
    own_points = first_row + jnp.arange(col_rows, dtype=jnp.int32)
    own_position = doc_position(own_points, doc_lengths)
    columns = lax.axis_size("p")
    ahead = [(i, i + 1) for i in range(columns - 1)]
    my_taps = lax.dynamic_slice_in_dim(short_taps, zh * half, half, 2)
    my_filter = lax.dynamic_slice_in_dim(filter_taps, zh * half, half, 1)
    my_decay = lax.dynamic_slice_in_dim(decay_rate, zh * half, half, 0)
    edge_rows = lax.ppermute(projected[col_rows - 2 :], "p", ahead)
    short_all = short_filter(
        jnp.concatenate([edge_rows, projected], 0), my_taps, own_position, col_rows
    )
    kv_product = (short_all[:, 1] * short_all[:, 2]).astype(jnp.bfloat16)
    tail_rows = lax.ppermute(kv_product[col_rows - tap_count :], "p", ahead)
    extended = jnp.concatenate([tail_rows, kv_product], 0)
    query = short_all[:, 0]
    shaped = my_filter * jnp.exp(
        -my_decay[None, :] * jnp.arange(tap_count, dtype=jnp.float32)[:, None]
    )
    long_mix = long_filter(extended, shaped, own_position, col_rows, tap_count)
    gated_mix = (query * long_mix).astype(jnp.bfloat16)
    summed = lax.psum_scatter(
        lax.dot_general(
            gated_mix, out_full, (((1,), (1,)), ((), ())), preferred_element_type=jnp.float32
        ).astype(jnp.bfloat16),
        COL,
        scatter_dimension=0,
        tiled=True,
    ).astype(jnp.float32)
    return (widened + summed).astype(jnp.bfloat16)


def solution(mesh):
    fsdp, tp = (mesh.shape["fsdp"], mesh.shape["tp"])
    grid = mesh.devices.reshape(fsdp // 2, 2, tp // 2, 2)
    fine = Mesh(grid, ("p", "zh", "zl", "c"))
    rows = ("p", "zh", "zl", "c")
    chan = ("zl", "c")
    in_specs = (
        P(rows, None),
        P(("p", "zh"), None, chan),
        P(("p", "zh"), chan),
        P(None, None, chan),
        P(None, chan),
        P(chan),
        P(),
    )
    out_specs = P(rows, None)
    return jax.shard_map(body, mesh=fine, in_specs=in_specs, out_specs=out_specs, check_vma=False)
```

profile of v0, /device:TPU:6, one launch (start us, length us, event | category | flops | bytes accessed | tf_op | source)
XLA Modules:
  0.0 328.6 jit_solution(9179054055207928626)
XLA Ops:
  6.5 1.1 fusion.25
  8.1 7.3 %collective-permute-start = (bf16[128,3,256]{0,2,1:T(8,128)(2,1)S(1)}, bf16[128,3,256]{0,2,1:T(8,128)(2,1)S(1)}, u32[]{:S(2)}, u32[]{:S(2)}) collective-permute-start(bf16[128,3,256]{0,2,1:T(8,128)(2,1)S(1)} %broadcast_select_fusion.2), channel_id=1, source_target_pairs={{0,8},{8,0},{1,9},{9,1},{2,10},{10,2},{3,11},{11,3},{4,12},{12,4},... | collective-permute-start | bytes 589832 | tf_op jit(solution)/shard_map/ppermute | solution.py:50
  15.3 5.0 %collective-permute-done = bf16[128,3,256]{0,2,1:T(8,128)(2,1)S(1)} collective-permute-done((bf16[128,3,256]{0,2,1:T(8,128)(2,1)S(1)}, bf16[128,3,256]{0,2,1:T(8,128)(2,1)S(1)}, u32[]{:S(2)}, u32[]{:S(2)}) %collective-permute-start) | collective-permute-done | bytes 196640 | tf_op jit(solution)/shard_map/ppermute | solution.py:50
  20.4 0.8 pad_maximum_fusion.2
  21.5 1.0 fusion.17
  22.5 9.2 %collective-permute-start.3 = (bf16[128,256]{1,0:T(8,128)(2,1)S(1)}, bf16[128,256]{1,0:T(8,128)(2,1)S(1)}, u32[]{:S(2)}, u32[]{:S(2)}) collective-permute-start(bf16[128,256]{1,0:T(8,128)(2,1)S(1)} %broadcast_select_fusion.6), channel_id=1, source_target_pairs={{0,8},{8,0},{1,9},{9,1},{2,10},{10,2},{3,11},{11,3},{4,12},{12,4},... | collective-permute-start | bytes 196616 | tf_op jit(solution)/shard_map/ppermute | solution.py:50
  32.4 1.9 collective-permute-done.3
  34.2 63.8 %all-gather.6.cloned.1.call-done = bf16[4096,3,256]{0,2,1:T(8,128)(2,1)} async-done(((bf16[256,3,256]{0,2,1:T(8,128)(2,1)}), bf16[4096,3,256]{0,2,1:T(8,128)(2,1)}) %all-gather.6.cloned.1.call-update) | async-done | bytes 6291472 | tf_op jit(solution)/shard_map/all_gather | solution.py:69
  98.0 57.4 %all-gather.4.cloned.1.call-done = bf16[1024,4096]{1,0:T(8,128)(2,1)} async-done(((bf16[64,4096]{1,0:T(8,128)(2,1)}), bf16[1024,4096]{1,0:T(8,128)(2,1)}) %all-gather.4.cloned.1.call-update) | async-done | bytes 8388624 | tf_op jit(solution)/shard_map/all_gather | solution.py:67
  155.4 11.0 %convolution_convert_fusion.1 = bf16[1024,768]{1,0:T(8,128)(2,1)S(1)} fusion(bf16[1024,4096]{1,0:T(8,128)(2,1)} %all-gather.4.cloned.1.call-done, bf16[4096,768]{0,1:T(8,128)(2,1)} %bitcast.91), kind=kOutput, calls=%fused_computation.52 | convolution fusion | flops 6443237376 | bytes 16252928 | tf_op jit(solution)/shard_map/dot_general | solution.py:73
  166.4 1.2 copy-done.3
  167.8 3.4 %collective-permute-start.1 = (bf16[2,3,256]{0,2,1:T(8,128)(2,1)S(1)}, bf16[2,3,256]{0,2,1:T(8,128)(2,1)S(1)}, u32[]{:S(2)}, u32[]{:S(2)}) collective-permute-start(bf16[2,3,256]{0,2,1:T(8,128)(2,1)S(1)} %bitcast.73), channel_id=1, source_target_pairs={{0,16},{16,32},{32,48},{48,64},{64,80},{80,96},{96,112},{112,128},... | collective-permute-start | bytes 9224 | tf_op jit(solution)/shard_map/ppermute | solution.py:83
  171.2 0.7 pad_maximum_fusion.3
  171.9 1.7 copy.22
  173.7 3.1 collective-permute-done.1
  176.8 2.3 select_add_fusion.1
  179.2 5.7 %collective-permute-start.2 = (bf16[128,256]{0,1:T(8,128)(2,1)S(1)}, bf16[128,256]{0,1:T(8,128)(2,1)S(1)}, u32[]{:S(2)}, u32[]{:S(2)}) collective-permute-start(bf16[128,256]{0,1:T(8,128)(2,1)S(1)} %slice_bitcast_fusion.1), channel_id=1, source_target_pairs={{0,16},{16,32},{32,48},{48,64},{64,80},{80,96},{96,112},{112,128},... | collective-permute-start | bytes 196616 | tf_op jit(solution)/shard_map/ppermute | solution.py:88
  185.0 1.6 collective-permute-done.2
  186.6 0.2 copy.24
  186.9 54.6 %while.17 = (s32[]{:T(128)}, f32[1024,256]{1,0:T(8,128)S(1)}, s32[1024]{0:T(1024)S(1)}, f32[128,256]{1,0:T(8,128)S(1)}, bf16[1152,256]{1,0:T(8,128)(2,1)S(1)}, /...) while((s32[]{:T(128)}, f32[1024,256]{1,0:T(8,128)S(1)}, ...), condition=%wide.region_4.5_spmd.clone, body=%wide.region_3.4_spmd.clone.sunk | while | flops 17055876 | bytes 10573783 | solution.py:41
  187.3 6.4 %fusion.31 = f32[1024,256]{1,0:T(8,128)S(1)} fusion(f32[1024,256]{1,0:T(8,128)S(1)} %get-tuple-element.431, bf16[1152,256]{1,0:T(8,128)(2,1)S(1)} %get-tuple-element.473, s32[]{:T(128)S(6)} %select_n.767, f32[256]{0:T(256)S(1)} %bitcast.75, s32[]{:T(128)S(6)} %select_n.784, f32[256]{0:T(256)S(1)} %bitcast.76, s32[]{:T(128)S(6)} %select_n.785, ...), kind=kLoop, calls=%fused_computation.15.clone.1 | loop fusion | flops 17039360 | bytes 10518593 | tf_op jit(solution)/shard_map/while/body/eval_jaxpr/add | solution.py:35
  194.1 6.4 %fusion.31 = f32[1024,256]{1,0:T(8,128)S(1)} fusion(f32[1024,256]{1,0:T(8,128)S(1)} %get-tuple-element.431, bf16[1152,256]{1,0:T(8,128)(2,1)S(1)} %get-tuple-element.473, s32[]{:T(128)S(6)} %select_n.767, f32[256]{0:T(256)S(1)} %bitcast.75, s32[]{:T(128)S(6)} %select_n.784, f32[256]{0:T(256)S(1)} %bitcast.76, s32[]{:T(128)S(6)} %select_n.785, ...), kind=kLoop, calls=%fused_computation.15.clone.1 | loop fusion | flops 17039360 | bytes 10518593 | tf_op jit(solution)/shard_map/while/body/eval_jaxpr/add | solution.py:35
  200.9 6.4 %fusion.31 = f32[1024,256]{1,0:T(8,128)S(1)} fusion(f32[1024,256]{1,0:T(8,128)S(1)} %get-tuple-element.431, bf16[1152,256]{1,0:T(8,128)(2,1)S(1)} %get-tuple-element.473, s32[]{:T(128)S(6)} %select_n.767, f32[256]{0:T(256)S(1)} %bitcast.75, s32[]{:T(128)S(6)} %select_n.784, f32[256]{0:T(256)S(1)} %bitcast.76, s32[]{:T(128)S(6)} %select_n.785, ...), kind=kLoop, calls=%fused_computation.15.clone.1 | loop fusion | flops 17039360 | bytes 10518593 | tf_op jit(solution)/shard_map/while/body/eval_jaxpr/add | solution.py:35
  207.8 6.4 %fusion.31 = f32[1024,256]{1,0:T(8,128)S(1)} fusion(f32[1024,256]{1,0:T(8,128)S(1)} %get-tuple-element.431, bf16[1152,256]{1,0:T(8,128)(2,1)S(1)} %get-tuple-element.473, s32[]{:T(128)S(6)} %select_n.767, f32[256]{0:T(256)S(1)} %bitcast.75, s32[]{:T(128)S(6)} %select_n.784, f32[256]{0:T(256)S(1)} %bitcast.76, s32[]{:T(128)S(6)} %select_n.785, ...), kind=kLoop, calls=%fused_computation.15.clone.1 | loop fusion | flops 17039360 | bytes 10518593 | tf_op jit(solution)/shard_map/while/body/eval_jaxpr/add | solution.py:35
  214.6 6.4 %fusion.31 = f32[1024,256]{1,0:T(8,128)S(1)} fusion(f32[1024,256]{1,0:T(8,128)S(1)} %get-tuple-element.431, bf16[1152,256]{1,0:T(8,128)(2,1)S(1)} %get-tuple-element.473, s32[]{:T(128)S(6)} %select_n.767, f32[256]{0:T(256)S(1)} %bitcast.75, s32[]{:T(128)S(6)} %select_n.784, f32[256]{0:T(256)S(1)} %bitcast.76, s32[]{:T(128)S(6)} %select_n.785, ...), kind=kLoop, calls=%fused_computation.15.clone.1 | loop fusion | flops 17039360 | bytes 10518593 | tf_op jit(solution)/shard_map/while/body/eval_jaxpr/add | solution.py:35
  221.4 6.4 %fusion.31 = f32[1024,256]{1,0:T(8,128)S(1)} fusion(f32[1024,256]{1,0:T(8,128)S(1)} %get-tuple-element.431, bf16[1152,256]{1,0:T(8,128)(2,1)S(1)} %get-tuple-element.473, s32[]{:T(128)S(6)} %select_n.767, f32[256]{0:T(256)S(1)} %bitcast.75, s32[]{:T(128)S(6)} %select_n.784, f32[256]{0:T(256)S(1)} %bitcast.76, s32[]{:T(128)S(6)} %select_n.785, ...), kind=kLoop, calls=%fused_computation.15.clone.1 | loop fusion | flops 17039360 | bytes 10518593 | tf_op jit(solution)/shard_map/while/body/eval_jaxpr/add | solution.py:35
  228.2 6.4 %fusion.31 = f32[1024,256]{1,0:T(8,128)S(1)} fusion(f32[1024,256]{1,0:T(8,128)S(1)} %get-tuple-element.431, bf16[1152,256]{1,0:T(8,128)(2,1)S(1)} %get-tuple-element.473, s32[]{:T(128)S(6)} %select_n.767, f32[256]{0:T(256)S(1)} %bitcast.75, s32[]{:T(128)S(6)} %select_n.784, f32[256]{0:T(256)S(1)} %bitcast.76, s32[]{:T(128)S(6)} %select_n.785, ...), kind=kLoop, calls=%fused_computation.15.clone.1 | loop fusion | flops 17039360 | bytes 10518593 | tf_op jit(solution)/shard_map/while/body/eval_jaxpr/add | solution.py:35
  235.1 6.4 %fusion.31 = f32[1024,256]{1,0:T(8,128)S(1)} fusion(f32[1024,256]{1,0:T(8,128)S(1)} %get-tuple-element.431, bf16[1152,256]{1,0:T(8,128)(2,1)S(1)} %get-tuple-element.473, s32[]{:T(128)S(6)} %select_n.767, f32[256]{0:T(256)S(1)} %bitcast.75, s32[]{:T(128)S(6)} %select_n.784, f32[256]{0:T(256)S(1)} %bitcast.76, s32[]{:T(128)S(6)} %select_n.785, ...), kind=kLoop, calls=%fused_computation.15.clone.1 | loop fusion | flops 17039360 | bytes 10518593 | tf_op jit(solution)/shard_map/while/body/eval_jaxpr/add | solution.py:35
  241.5 0.3 copy.25
  241.9 7.6 %convolution_convert_fusion = bf16[1024,4096]{1,0:T(8,128)(2,1)} fusion(bf16[4096,256]{1,0:T(8,128)(2,1)} %all-gather.8.cloned.1.call-done, f32[1024,256]{0,1:T(8,128)S(1)} %copy.25, f32[1024,3,256]{0,2,1:T(8,128)} %copy-done), kind=kOutput, calls=%fused_computation.48 | convolution fusion | flops 2152202240 | bytes 12582912 | tf_op jit(solution)/shard_map/dot_general | solution.py:97
  249.5 70.6 %reduce-scatter.2.cloned.1.call-done = bf16[64,4096]{1,0:T(8,128)(2,1)} async-done(((bf16[1024,4096]{1,0:T(8,128)(2,1)}), bf16[64,4096]{1,0:T(8,128)(2,1)}) %reduce-scatter.2.cloned.1.call-update) | async-done | bytes 524304 | tf_op jit(solution)/shard_map/reduce_scatter | solution.py:96
  320.1 2.0 fusion.18
  (68 shorter events, 3.0 us)
Async XLA Ops:
  6.5 14.7 %copy-start.1 = (bf16[64,4096]{1,0:T(8,128)(2,1)S(1)}, bf16[64,4096]{1,0:T(8,128)(2,1)}, u32[]{:S(2)}) copy-start(bf16[64,4096]{1,0:T(8,128)(2,1)} %param.9) | copy-start | bytes 1572868
  6.5 91.5 %all-gather.6.cloned.1.call-start = ((), (), s32[]{:S(2)}) async-start(), calls=%async_computation.2 | async-start | bytes 6684672 | tf_op jit(solution)/shard_map/all_gather | solution.py:69
  6.5 16.0 %copy-start.4 = (bf16[128,512]{1,0:T(8,128)(2,1)S(1)}, bf16[128,512]{1,0:T(8,128)(2,1)}, u32[]{:S(2)}) copy-start(bf16[128,512]{1,0:T(8,128)(2,1)} %param.11) | copy-start | bytes 393220
  6.5 25.2 %copy-start.7 = (s32[64]{0:T(128)S(1)}, s32[64]{0:T(128)}, u32[]{:S(2)}) copy-start(s32[64]{0:T(128)} %param.15) | copy-start | bytes 772
  7.7 24.4 %copy-start.8 = (f32[512]{0:T(512)S(1)}, f32[512]{0:T(512)}, u32[]{:S(2)}) copy-start(f32[512]{0:T(512)} %param.14) | copy-start | bytes 6148
  7.7 24.6 %copy-start.5 = (f32[128,512]{1,0:T(8,128)S(1)}, f32[128,512]{1,0:T(8,128)}, u32[]{:S(2)}) copy-start(f32[128,512]{1,0:T(8,128)} %param.13) | copy-start | bytes 786436
  7.7 24.6 %copy-start.6 = (f32[3,3,512]{2,1,0:T(4,128)S(1)}, f32[3,3,512]{2,1,0:T(4,128)}, u32[]{:S(2)}) copy-start(f32[3,3,512]{2,1,0:T(4,128)} %param.12) | copy-start | bytes 55300
  8.1 12.3 %collective-permute-start = (bf16[128,3,256]{0,2,1:T(8,128)(2,1)S(1)}, bf16[128,3,256]{0,2,1:T(8,128)(2,1)S(1)}, u32[]{:S(2)}, u32[]{:S(2)}) collective-permute-start(bf16[128,3,256]{0,2,1:T(8,128)(2,1)S(1)} %broadcast_select_fusion.2), channel_id=1, source_target_pairs={{0,8},{8,0},{1,9},{9,1},{2,10},{10,2},{3,11},{11,3},{4,12},{12,4},... | collective-permute-start | bytes 589832 | tf_op jit(solution)/shard_map/ppermute | solution.py:50
  21.2 134.2 %all-gather.4.cloned.1.call-start = ((), (), s32[]{:S(2)}) async-start(), calls=%async_computation.1 | async-start | bytes 8912896 | tf_op jit(solution)/shard_map/all_gather | solution.py:67
  22.5 219.4 %all-gather.8.cloned.1.call-start = ((), (), s32[]{:S(2)}) async-start(), calls=%async_computation.3 | async-start | bytes 2228224 | tf_op jit(solution)/shard_map/all_gather | solution.py:71
  22.5 11.7 %collective-permute-start.3 = (bf16[128,256]{1,0:T(8,128)(2,1)S(1)}, bf16[128,256]{1,0:T(8,128)(2,1)S(1)}, u32[]{:S(2)}, u32[]{:S(2)}) collective-permute-start(bf16[128,256]{1,0:T(8,128)(2,1)S(1)} %broadcast_select_fusion.6), channel_id=1, source_target_pairs={{0,8},{8,0},{1,9},{9,1},{2,10},{10,2},{3,11},{11,3},{4,12},{12,4},... | collective-permute-start | bytes 196616 | tf_op jit(solution)/shard_map/ppermute | solution.py:50
  166.4 1.2 copy-start.3
  167.8 8.9 %collective-permute-start.1 = (bf16[2,3,256]{0,2,1:T(8,128)(2,1)S(1)}, bf16[2,3,256]{0,2,1:T(8,128)(2,1)S(1)}, u32[]{:S(2)}, u32[]{:S(2)}) collective-permute-start(bf16[2,3,256]{0,2,1:T(8,128)(2,1)S(1)} %bitcast.73), channel_id=1, source_target_pairs={{0,16},{16,32},{32,48},{48,64},{64,80},{80,96},{96,112},{112,128},... | collective-permute-start | bytes 9224 | tf_op jit(solution)/shard_map/ppermute | solution.py:83
  171.9 148.2 %reduce-scatter.2.cloned.1.call-start = ((), (), s32[]{:S(2)}) async-start(), calls=%async_computation.4 | async-start | bytes 8912896 | tf_op jit(solution)/shard_map/reduce_scatter | solution.py:96
  179.0 7.6 %copy-start = (f32[1024,3,256]{0,2,1:T(8,128)}, f32[1024,3,256]{0,2,1:T(8,128)S(1)}, u32[]{:S(2)}) copy-start(f32[1024,3,256]{0,2,1:T(8,128)S(1)} %select_add_fusion.1) | copy-start | bytes 9437188
  179.2 7.4 %collective-permute-start.2 = (bf16[128,256]{0,1:T(8,128)(2,1)S(1)}, bf16[128,256]{0,1:T(8,128)(2,1)S(1)}, u32[]{:S(2)}, u32[]{:S(2)}) collective-permute-start(bf16[128,256]{0,1:T(8,128)(2,1)S(1)} %slice_bitcast_fusion.1), channel_id=1, source_target_pairs={{0,16},{16,32},{32,48},{48,64},{64,80},{80,96},{96,112},{112,128},... | collective-permute-start | bytes 196616 | tf_op jit(solution)/shard_map/ppermute | solution.py:88
  249.4 70.6 %copy-start.2 = (bf16[64,4096]{1,0:T(8,128)(2,1)S(1)}, bf16[64,4096]{1,0:T(8,128)(2,1)}, u32[]{:S(2)}) copy-start(bf16[64,4096]{1,0:T(8,128)(2,1)} %param.9) | copy-start | bytes 1572868
Sparse Core Ops, SparseCore 0:
  21.3 76.6 all-gather.5
  99.8 55.5 all-gather.3
  172.0 47.8 all-gather.7
  249.6 70.4 reduce-scatter.1
where the time goes:
time: 329 us
  waiting for transfers between devices  203 us (62%)
  other arithmetic  59.4 us (18%)
  starting transfers between devices  25.6 us (8%)
  matrix products  18.6 us (6%)
  between operations  13.4 us (4%)
  local copies, waits for them, and re-layouts  5.96 us (2%)
    reduce_scatter x1, waiting for transfers between devices, body(): lax.psum_scatter(lax.dot_general(gated_mix, out_full, (((1,), (1,)), ((),...  70.6 us
    all_gather x1, waiting for transfers between devices, body(): in_full = lax.all_gather(in_piece, 'p', axis=0, tiled=True)  63.8 us
    all_gather x1, waiting for transfers between devices, body(): gathered = lax.all_gather(normed, COL, axis=0, tiled=True)  57.4 us
    add x8, other arithmetic, tap_group(): running + jnp.where(inside, weight_row * window.astype(jnp.float32), jnp....  51.3 us
    ppermute x2, starting transfers between devices, swap_half(): got = lax.ppermute(give, 'zh', [(0, 1), (1, 0)])  16.4 us
    dot_general x1, matrix products, body(): projected = jnp.dot(gathered, flat_in, preferred_element_type=jnp.float32)  11 us
    dot_general x1, matrix products, body(): lax.dot_general(gated_mix, out_full, (((1,), (1,)), ((), ())), preferred_...  7.58 us
    ppermute x2, waiting for transfers between devices, swap_half(): got = lax.ppermute(give, 'zh', [(0, 1), (1, 0)])  6.86 us
  transfers between devices with their start and end apart: 8, of which 7 were waited for; matrix products, arithmetic and copies ran while one was open for 18% of the time, Pallas kernels for 0%

commit v1 on v0

--- a/solution.py
+++ b/solution.py
@@ -64,7 +64,10 @@
     normed = (
         widened * lax.rsqrt(jnp.mean(widened * widened, axis=1, keepdims=True) + 1e-06)
     ).astype(jnp.bfloat16)
-    gathered = lax.all_gather(normed, COL, axis=0, tiled=True)
+    size = lax.axis_size(COL)
+    blocks = jnp.stack([normed for _ in range(size)])
+    blocks = lax.all_to_all(blocks, COL, split_axis=0, concat_axis=0)
+    gathered = jnp.concatenate(blocks, axis=0)
     in_piece = swap_half(in_weight, zh, 2)
     in_full = lax.all_gather(in_piece, "p", axis=0, tiled=True)
     out_piece = swap_half(out_weight, zh, 1)

time: 329 us -> 461 us (1.40)
  waiting for transfers between devices: 203 us -> 332 us
    ppermute x2, waiting for transfers between devices: 6.86 us -> 195 us  [swap_half(): got = lax.ppermute(give, 'zh', [(0, 1), (1, 0)])]
    all_gather x1 -> x0, waiting for transfers between devices: 57.4 us -> none  [body(): gathered = lax.all_gather(normed, COL, axis=0, tiled=True)]
    ppermute x2, starting transfers between devices: 16.4 us -> 6.39 us  [swap_half(): got = lax.ppermute(give, 'zh', [(0, 1), (1, 0)])]
    all_to_all x0 -> x1, starting transfers between devices: none -> 8.75 us  [body(): blocks = lax.all_to_all(blocks, COL, split_axis=0, concat_axis=0)]
  transfers between devices with their start and end apart: 8 -> 8, of which waited for: 7 -> 6; matrix products, arithmetic and copies ran while one was open for 18% -> 13% of each run, Pallas kernels for 0% -> 0%
where the time goes in v1:
time: 461 us; the launch traced here: 460 us
  waiting for transfers between devices  332 us (72%)
  other arithmetic  60.7 us (13%)
  starting transfers between devices  24.3 us (5%)
  matrix products  18.6 us (4%)
  between operations  13.4 us (3%)
  local copies, waits for them, and re-layouts  9.21 us (2%)
    ppermute x2, waiting for transfers between devices, swap_half(): got = lax.ppermute(give, 'zh', [(0, 1), (1, 0)])  195 us
    reduce_scatter x1, waiting for transfers between devices, body(): lax.psum_scatter(lax.dot_general(gated_mix, out_full, (((1,), (1,)), ((),...  72.7 us
    all_gather x1, waiting for transfers between devices, body(): in_full = lax.all_gather(in_piece, 'p', axis=0, tiled=True)  61 us
    add x8, other arithmetic, tap_group(): running + jnp.where(inside, weight_row * window.astype(jnp.float32), jnp....  51.4 us
    dot_general x1, matrix products, body(): projected = jnp.dot(gathered, flat_in, preferred_element_type=jnp.float32)  11 us
  transfers between devices with their start and end apart: 8, of which 6 were waited for; matrix products, arithmetic and copies ran while one was open for 13% of the time, Pallas kernels for 0%

profile of v1, /device:TPU:6, one launch (start us, length us, event | category | flops | bytes accessed | tf_op | source)
XLA Modules:
  0.0 460.2 jit_solution(17635867757282137895)
XLA Ops:
  6.5 1.2 fusion.16
  7.8 1.2 fusion.17
  9.0 4.3 stack.2
  13.3 8.8 %all-to-all-start = ((bf16[16,64,4096]{2,1,0:T(8,128)(2,1)}), bf16[16,64,4096]{2,1,0:T(8,128)(2,1)}, u32[]{:S(2)}, u32[]{:S(2)}) async-start(bf16[16,64,4096]{2,1,0:T(8,128)(2,1)} %stack.2), calls=%async_computation | async-start | bytes 16777216 | tf_op jit(solution)/shard_map/all_to_all | solution.py:69
  22.6 5.9 %collective-permute-start = (bf16[128,3,256]{0,2,1:T(8,128)(2,1)S(1)}, bf16[128,3,256]{0,2,1:T(8,128)(2,1)S(1)}, u32[]{:S(2)}, u32[]{:S(2)}) collective-permute-start(bf16[128,3,256]{0,2,1:T(8,128)(2,1)S(1)} %broadcast_select_fusion.2), channel_id=1, source_target_pairs={{0,8},{8,0},{1,9},{9,1},{2,10},{10,2},{3,11},{11,3},{4,12},{12,4},... | collective-permute-start | bytes 589832 | tf_op jit(solution)/shard_map/ppermute | solution.py:50
  28.5 186.9 %collective-permute-done = bf16[128,3,256]{0,2,1:T(8,128)(2,1)S(1)} collective-permute-done((bf16[128,3,256]{0,2,1:T(8,128)(2,1)S(1)}, bf16[128,3,256]{0,2,1:T(8,128)(2,1)S(1)}, u32[]{:S(2)}, u32[]{:S(2)}) %collective-permute-start) | collective-permute-done | bytes 196640 | tf_op jit(solution)/shard_map/ppermute | solution.py:50
  215.4 0.8 pad_maximum_fusion.2
  216.3 0.5 collective-permute-start.3
  217.5 7.8 %collective-permute-done.3 = bf16[128,256]{1,0:T(8,128)(2,1)S(1)} collective-permute-done((bf16[128,256]{1,0:T(8,128)(2,1)S(1)}, bf16[128,256]{1,0:T(8,128)(2,1)S(1)}, u32[]{:S(2)}, u32[]{:S(2)}) %collective-permute-start.3) | collective-permute-done | bytes 65568 | tf_op jit(solution)/shard_map/ppermute | solution.py:50
  225.3 61.0 %all-gather.3.cloned.1.call-done = bf16[4096,3,256]{0,2,1:T(8,128)(2,1)} async-done(((bf16[256,3,256]{0,2,1:T(8,128)(2,1)}), bf16[4096,3,256]{0,2,1:T(8,128)(2,1)}) %all-gather.3.cloned.1.call-update) | async-done | bytes 6291472 | tf_op jit(solution)/shard_map/all_gather | solution.py:72
  286.4 11.0 %convolution_convert_fusion.1 = bf16[1024,768]{1,0:T(8,128)(2,1)S(1)} fusion(bf16[1024,4096]{1,0:T(8,128)(2,1)} %bitcast.2, bf16[4096,768]{0,1:T(8,128)(2,1)} %bitcast.92), kind=kOutput, calls=%fused_computation.52 | convolution fusion | flops 6443237376 | bytes 16252928 | tf_op jit(solution)/shard_map/dot_general | solution.py:76
  297.4 1.2 copy-done.2
  298.7 3.4 collective-permute-start.1
  302.1 0.7 pad_maximum_fusion.3
  302.8 1.7 copy.22
  304.6 1.7 collective-permute-done.1
  306.3 2.3 select_add_fusion.1
  308.8 5.6 %collective-permute-start.2 = (bf16[128,256]{0,1:T(8,128)(2,1)S(1)}, bf16[128,256]{0,1:T(8,128)(2,1)S(1)}, u32[]{:S(2)}, u32[]{:S(2)}) collective-permute-start(bf16[128,256]{0,1:T(8,128)(2,1)S(1)} %slice_bitcast_fusion.1), channel_id=1, source_target_pairs={{0,16},{16,32},{32,48},{48,64},{64,80},{80,96},{96,112},{112,128},... | collective-permute-start | bytes 196616 | tf_op jit(solution)/shard_map/ppermute | solution.py:91
  314.5 1.6 collective-permute-done.2
  316.4 54.6 %while.17 = (s32[]{:T(128)}, f32[1024,256]{1,0:T(8,128)S(1)}, s32[1024]{0:T(1024)S(1)}, f32[128,256]{1,0:T(8,128)S(1)}, bf16[1152,256]{1,0:T(8,128)(2,1)S(1)}, /...) while((s32[]{:T(128)}, f32[1024,256]{1,0:T(8,128)S(1)}, ...), condition=%wide.region_4.5_spmd.clone, body=%wide.region_3.4_spmd.clone.sunk | while | flops 17055876 | bytes 10573791 | solution.py:41
  316.8 6.4 %fusion.31 = f32[1024,256]{1,0:T(8,128)S(1)} fusion(f32[1024,256]{1,0:T(8,128)S(1)} %get-tuple-element.431, bf16[1152,256]{1,0:T(8,128)(2,1)S(1)} %get-tuple-element.473, s32[]{:T(128)S(6)} %select_n.767, f32[256]{0:T(256)S(1)} %bitcast.76, s32[]{:T(128)S(6)} %select_n.784, f32[256]{0:T(256)S(1)} %bitcast.77, s32[]{:T(128)S(6)} %select_n.785, ...), kind=kLoop, calls=%fused_computation.15.clone.1 | loop fusion | flops 17039360 | bytes 10518593 | tf_op jit(solution)/shard_map/while/body/eval_jaxpr/add | solution.py:35
  323.7 6.4 %fusion.31 = f32[1024,256]{1,0:T(8,128)S(1)} fusion(f32[1024,256]{1,0:T(8,128)S(1)} %get-tuple-element.431, bf16[1152,256]{1,0:T(8,128)(2,1)S(1)} %get-tuple-element.473, s32[]{:T(128)S(6)} %select_n.767, f32[256]{0:T(256)S(1)} %bitcast.76, s32[]{:T(128)S(6)} %select_n.784, f32[256]{0:T(256)S(1)} %bitcast.77, s32[]{:T(128)S(6)} %select_n.785, ...), kind=kLoop, calls=%fused_computation.15.clone.1 | loop fusion | flops 17039360 | bytes 10518593 | tf_op jit(solution)/shard_map/while/body/eval_jaxpr/add | solution.py:35
  330.5 6.4 %fusion.31 = f32[1024,256]{1,0:T(8,128)S(1)} fusion(f32[1024,256]{1,0:T(8,128)S(1)} %get-tuple-element.431, bf16[1152,256]{1,0:T(8,128)(2,1)S(1)} %get-tuple-element.473, s32[]{:T(128)S(6)} %select_n.767, f32[256]{0:T(256)S(1)} %bitcast.76, s32[]{:T(128)S(6)} %select_n.784, f32[256]{0:T(256)S(1)} %bitcast.77, s32[]{:T(128)S(6)} %select_n.785, ...), kind=kLoop, calls=%fused_computation.15.clone.1 | loop fusion | flops 17039360 | bytes 10518593 | tf_op jit(solution)/shard_map/while/body/eval_jaxpr/add | solution.py:35
  337.3 6.4 %fusion.31 = f32[1024,256]{1,0:T(8,128)S(1)} fusion(f32[1024,256]{1,0:T(8,128)S(1)} %get-tuple-element.431, bf16[1152,256]{1,0:T(8,128)(2,1)S(1)} %get-tuple-element.473, s32[]{:T(128)S(6)} %select_n.767, f32[256]{0:T(256)S(1)} %bitcast.76, s32[]{:T(128)S(6)} %select_n.784, f32[256]{0:T(256)S(1)} %bitcast.77, s32[]{:T(128)S(6)} %select_n.785, ...), kind=kLoop, calls=%fused_computation.15.clone.1 | loop fusion | flops 17039360 | bytes 10518593 | tf_op jit(solution)/shard_map/while/body/eval_jaxpr/add | solution.py:35
  344.1 6.4 %fusion.31 = f32[1024,256]{1,0:T(8,128)S(1)} fusion(f32[1024,256]{1,0:T(8,128)S(1)} %get-tuple-element.431, bf16[1152,256]{1,0:T(8,128)(2,1)S(1)} %get-tuple-element.473, s32[]{:T(128)S(6)} %select_n.767, f32[256]{0:T(256)S(1)} %bitcast.76, s32[]{:T(128)S(6)} %select_n.784, f32[256]{0:T(256)S(1)} %bitcast.77, s32[]{:T(128)S(6)} %select_n.785, ...), kind=kLoop, calls=%fused_computation.15.clone.1 | loop fusion | flops 17039360 | bytes 10518593 | tf_op jit(solution)/shard_map/while/body/eval_jaxpr/add | solution.py:35
  351.0 6.4 %fusion.31 = f32[1024,256]{1,0:T(8,128)S(1)} fusion(f32[1024,256]{1,0:T(8,128)S(1)} %get-tuple-element.431, bf16[1152,256]{1,0:T(8,128)(2,1)S(1)} %get-tuple-element.473, s32[]{:T(128)S(6)} %select_n.767, f32[256]{0:T(256)S(1)} %bitcast.76, s32[]{:T(128)S(6)} %select_n.784, f32[256]{0:T(256)S(1)} %bitcast.77, s32[]{:T(128)S(6)} %select_n.785, ...), kind=kLoop, calls=%fused_computation.15.clone.1 | loop fusion | flops 17039360 | bytes 10518593 | tf_op jit(solution)/shard_map/while/body/eval_jaxpr/add | solution.py:35
  357.8 6.4 %fusion.31 = f32[1024,256]{1,0:T(8,128)S(1)} fusion(f32[1024,256]{1,0:T(8,128)S(1)} %get-tuple-element.431, bf16[1152,256]{1,0:T(8,128)(2,1)S(1)} %get-tuple-element.473, s32[]{:T(128)S(6)} %select_n.767, f32[256]{0:T(256)S(1)} %bitcast.76, s32[]{:T(128)S(6)} %select_n.784, f32[256]{0:T(256)S(1)} %bitcast.77, s32[]{:T(128)S(6)} %select_n.785, ...), kind=kLoop, calls=%fused_computation.15.clone.1 | loop fusion | flops 17039360 | bytes 10518593 | tf_op jit(solution)/shard_map/while/body/eval_jaxpr/add | solution.py:35
  364.6 6.4 %fusion.31 = f32[1024,256]{1,0:T(8,128)S(1)} fusion(f32[1024,256]{1,0:T(8,128)S(1)} %get-tuple-element.431, bf16[1152,256]{1,0:T(8,128)(2,1)S(1)} %get-tuple-element.473, s32[]{:T(128)S(6)} %select_n.767, f32[256]{0:T(256)S(1)} %bitcast.76, s32[]{:T(128)S(6)} %select_n.784, f32[256]{0:T(256)S(1)} %bitcast.77, s32[]{:T(128)S(6)} %select_n.785, ...), kind=kLoop, calls=%fused_computation.15.clone.1 | loop fusion | flops 17039360 | bytes 10518593 | tf_op jit(solution)/shard_map/while/body/eval_jaxpr/add | solution.py:35
  371.1 0.3 copy.25
  371.4 7.6 %convolution_convert_fusion = bf16[1024,4096]{1,0:T(8,128)(2,1)} fusion(bf16[4096,256]{1,0:T(8,128)(2,1)} %all-gather.5.cloned.1.call-done, f32[1024,256]{0,1:T(8,128)S(1)} %copy.25, f32[1024,3,256]{0,2,1:T(8,128)} %copy-done), kind=kOutput, calls=%fused_computation.48 | convolution fusion | flops 2152202240 | bytes 12582912 | tf_op jit(solution)/shard_map/dot_general | solution.py:100
  379.0 72.7 %reduce-scatter.2.cloned.1.call-done = bf16[64,4096]{1,0:T(8,128)(2,1)} async-done(((bf16[1024,4096]{1,0:T(8,128)(2,1)}), bf16[64,4096]{1,0:T(8,128)(2,1)}) %reduce-scatter.2.cloned.1.call-update) | async-done | bytes 524304 | tf_op jit(solution)/shard_map/reduce_scatter | solution.py:99
  451.7 2.0 fusion.18
  (68 shorter events, 3.1 us)
Async XLA Ops:
  13.3 8.9 %copy-start.4 = (bf16[128,3,512]{2,0,1:T(8,128)(2,1)S(1)}, bf16[128,3,512]{2,0,1:T(8,128)(2,1)}, u32[]{:S(2)}) copy-start(bf16[128,3,512]{2,0,1:T(8,128)(2,1)} %param.10) | copy-start | bytes 1179652
  13.3 273.0 %all-to-all-start = ((bf16[16,64,4096]{2,1,0:T(8,128)(2,1)}), bf16[16,64,4096]{2,1,0:T(8,128)(2,1)}, u32[]{:S(2)}, u32[]{:S(2)}) async-start(bf16[16,64,4096]{2,1,0:T(8,128)(2,1)} %stack.2), calls=%async_computation | async-start | bytes 16777216 | tf_op jit(solution)/shard_map/all_to_all | solution.py:69
  22.1 194.2 %copy-start.3 = (bf16[128,512]{1,0:T(8,128)(2,1)S(1)}, bf16[128,512]{1,0:T(8,128)(2,1)}, u32[]{:S(2)}) copy-start(bf16[128,512]{1,0:T(8,128)(2,1)} %param.11) | copy-start | bytes 393220
  22.1 194.8 %copy-start.7 = (s32[64]{0:T(128)S(1)}, s32[64]{0:T(128)}, u32[]{:S(2)}) copy-start(s32[64]{0:T(128)} %param.15) | copy-start | bytes 772
  22.1 195.1 %copy-start.8 = (f32[512]{0:T(512)S(1)}, f32[512]{0:T(512)}, u32[]{:S(2)}) copy-start(f32[512]{0:T(512)} %param.14) | copy-start | bytes 6148
  22.1 195.3 %copy-start.5 = (f32[128,512]{1,0:T(8,128)S(1)}, f32[128,512]{1,0:T(8,128)}, u32[]{:S(2)}) copy-start(f32[128,512]{1,0:T(8,128)} %param.13) | copy-start | bytes 786436
  22.1 195.4 %copy-start.6 = (f32[3,3,512]{2,1,0:T(4,128)S(1)}, f32[3,3,512]{2,1,0:T(4,128)}, u32[]{:S(2)}) copy-start(f32[3,3,512]{2,1,0:T(4,128)} %param.12) | copy-start | bytes 55300
  22.1 264.2 %all-gather.3.cloned.1.call-start = ((), (), s32[]{:S(2)}) async-start(), calls=%async_computation.2 | async-start | bytes 6684672 | tf_op jit(solution)/shard_map/all_gather | solution.py:72
  22.6 192.8 %collective-permute-start = (bf16[128,3,256]{0,2,1:T(8,128)(2,1)S(1)}, bf16[128,3,256]{0,2,1:T(8,128)(2,1)S(1)}, u32[]{:S(2)}, u32[]{:S(2)}) collective-permute-start(bf16[128,3,256]{0,2,1:T(8,128)(2,1)S(1)} %broadcast_select_fusion.2), channel_id=1, source_target_pairs={{0,8},{8,0},{1,9},{9,1},{2,10},{10,2},{3,11},{11,3},{4,12},{12,4},... | collective-permute-start | bytes 589832 | tf_op jit(solution)/shard_map/ppermute | solution.py:50
  216.3 155.2 %all-gather.5.cloned.1.call-start = ((), (), s32[]{:S(2)}) async-start(), calls=%async_computation.3 | async-start | bytes 2228224 | tf_op jit(solution)/shard_map/all_gather | solution.py:74
  216.3 9.0 %collective-permute-start.3 = (bf16[128,256]{1,0:T(8,128)(2,1)S(1)}, bf16[128,256]{1,0:T(8,128)(2,1)S(1)}, u32[]{:S(2)}, u32[]{:S(2)}) collective-permute-start(bf16[128,256]{1,0:T(8,128)(2,1)S(1)} %broadcast_select_fusion.6), channel_id=1, source_target_pairs={{0,8},{8,0},{1,9},{9,1},{2,10},{10,2},{3,11},{11,3},{4,12},{12,4},... | collective-permute-start | bytes 196616 | tf_op jit(solution)/shard_map/ppermute | solution.py:50
  297.4 1.2 copy-start.2
  298.7 7.6 %collective-permute-start.1 = (bf16[2,3,256]{0,2,1:T(8,128)(2,1)S(1)}, bf16[2,3,256]{0,2,1:T(8,128)(2,1)S(1)}, u32[]{:S(2)}, u32[]{:S(2)}) collective-permute-start(bf16[2,3,256]{0,2,1:T(8,128)(2,1)S(1)} %bitcast.74), channel_id=1, source_target_pairs={{0,16},{16,32},{32,48},{48,64},{64,80},{80,96},{96,112},{112,128},... | collective-permute-start | bytes 9224 | tf_op jit(solution)/shard_map/ppermute | solution.py:86
  302.8 148.9 %reduce-scatter.2.cloned.1.call-start = ((), (), s32[]{:S(2)}) async-start(), calls=%async_computation.4 | async-start | bytes 8912896 | tf_op jit(solution)/shard_map/reduce_scatter | solution.py:99
  308.6 7.5 %copy-start = (f32[1024,3,256]{0,2,1:T(8,128)}, f32[1024,3,256]{0,2,1:T(8,128)S(1)}, u32[]{:S(2)}) copy-start(f32[1024,3,256]{0,2,1:T(8,128)S(1)} %select_add_fusion.1) | copy-start | bytes 9437188
  308.8 7.4 %collective-permute-start.2 = (bf16[128,256]{0,1:T(8,128)(2,1)S(1)}, bf16[128,256]{0,1:T(8,128)(2,1)S(1)}, u32[]{:S(2)}, u32[]{:S(2)}) collective-permute-start(bf16[128,256]{0,1:T(8,128)(2,1)S(1)} %slice_bitcast_fusion.1), channel_id=1, source_target_pairs={{0,16},{16,32},{32,48},{48,64},{64,80},{80,96},{96,112},{112,128},... | collective-permute-start | bytes 196616 | tf_op jit(solution)/shard_map/ppermute | solution.py:91
  379.0 72.7 %copy-start.1 = (bf16[64,4096]{1,0:T(8,128)(2,1)S(1)}, bf16[64,4096]{1,0:T(8,128)(2,1)}, u32[]{:S(2)}) copy-start(bf16[64,4096]{1,0:T(8,128)(2,1)} %param.9) | copy-start | bytes 1572868
Sparse Core Ops, SparseCore 0:
  216.4 69.9 all-gather.2
  302.9 50.3 all-gather.4
  379.2 72.5 reduce-scatter.1
